TPU v7x, 256 devices: a whole 4x4x8 slice. The times are simulated.
256 devices in a mesh: section: 4 (over y), dp: 64 (over x, z, core).
Axes of the slice: x: 4, y: 4, z: 8, core: 2. Of those that a mesh axis runs over, the one named last changes fastest.
Arguments:
- grad_out: bfloat16 [12288, 1536], P('dp'), may hold values from -6 to 6
- section_inputs: bfloat16 [4, 12288, 1536], P('section', 'dp'), may hold values from -16 to 16
- lengths: int32 [256], replicated, may hold values from 1 to 48, 9216 in all
- bucket_list: int32 [256], P('dp'), may hold values from 0 to 255, each once
- conv_weight: float32 [4, 31, 1536], P('section'), may hold values from -8 to 8
- norm_gain: float32 [4, 1536], P('section'), may hold values from 0.5 to 1.5
- projection: bfloat16 [4, 1536, 1536], P('section'), may hold values from -0.15625 to 0.15625
Outputs:
- section_grads: bfloat16 [4, 12288, 1536], P('section', 'dp')
- projection_grad: float32 [4, 1536, 1536], P('section', 'dp')
- conv_grad: float32 [4, 31, 1536], P('section', None, 'dp')
- gain_grad: float32 [4, 1536], P('section', 'dp')
All inputs are finite; a program needn't handle non-finite values.
Results may differ from a plain program's by a relative error of at most 0.0057.
Values may be sent and summed in bfloat16 or wider, within the bound.
No kernel may reach another device: no remote copies, remote signals or barrier semaphores. Data moves between devices by JAX's collectives and lax.ppermute only.
A program may use at most 128 MiB of HBM per device.

v0:
```python
import jax
import jax.numpy as jnp
from jax import lax
from jax.sharding import PartitionSpec as P

eps = 1e-05


def from_behind(value, axis, by):
    size = lax.axis_size(axis)
    pairs = [(i, i + by) for i in range(size) if 0 <= i + by < size]
    return lax.ppermute(value, axis, pairs)


def layer_backward(x, dy, mask, kernel, gain, proj):
    taps = kernel.shape[0]
    half = (taps - 1) // 2
    frames = x.shape[0]
    u = x.astype(jnp.float32) * mask
    upad = jnp.pad(u, ((half, half), (0, 0)))
    a = jnp.zeros(u.shape, jnp.float32)
    for j in range(taps):
        a = a + kernel[j] * upad[j : j + frames]
    mean = jnp.mean(a, axis=-1, keepdims=True)
    cen = a - mean
    var = jnp.mean(cen * cen, axis=-1, keepdims=True)
    inv = lax.rsqrt(var + eps)
    nhat = cen * inv
    n = nhat * gain
    sig = jax.nn.sigmoid(n)
    h = (n * sig).astype(jnp.bfloat16)
    dz = (dy.astype(jnp.float32) * mask).astype(jnp.bfloat16)
    dh = lax.dot_general(dz, proj, (((1,), (1,)), ((), ())), preferred_element_type=jnp.float32)
    dn = dh * (sig + n * sig * (1.0 - sig))
    dgain = jnp.sum(dn * nhat, axis=0)
    dnh = dn * gain
    da = inv * (
        dnh
        - jnp.mean(dnh, axis=-1, keepdims=True)
        - nhat * jnp.mean(dnh * nhat, axis=-1, keepdims=True)
    )
    dapad = jnp.pad(da, ((half, half), (0, 0)))
    du = jnp.zeros(u.shape, jnp.float32)
    for j in range(taps):
        du = du + kernel[j] * dapad[2 * half - j : 2 * half - j + frames]
    dconv = jnp.stack([jnp.sum(da * upad[j : j + frames], axis=0) for j in range(taps)])
    dx = (dy.astype(jnp.float32) + mask * du).astype(jnp.bfloat16)
    return (dx, h, dz, dgain, dconv)


def body(grad_out, section_inputs, lengths, bucket_list, conv_weight, norm_gain, projection):
    sections = lax.axis_size("section")
    groups = lax.axis_size("dp")
    rank = lax.axis_index("section")
    micro = bucket_list.shape[0]
    rows, width = grad_out.shape
    frames = rows // micro
    table = jnp.arange(lengths.shape[0], dtype=jnp.int32)
    lens = jnp.sum(jnp.where(bucket_list[:, None] == table[None, :], lengths[None, :], 0), axis=1)
    masks = (jnp.arange(frames, dtype=jnp.int32)[None, :] < lens[:, None]).astype(jnp.float32)[
        ..., None
    ]
    saved = section_inputs[0].reshape(micro, frames, width)
    top = grad_out.reshape(micro, frames, width)
    kernel = conv_weight[0]
    gain = norm_gain[0]
    proj = projection[0]
    empty = jnp.zeros((micro, frames, width), jnp.bfloat16)
    buffers = (
        empty,
        empty,
        empty,
        jnp.zeros((width,), jnp.float32),
        jnp.zeros(kernel.shape, jnp.float32),
    )
    incoming = jnp.zeros((frames, width), jnp.bfloat16)
    ticks = micro + sections - 1
    for tick in range(ticks):
        slot = tick - (sections - 1 - rank)
        active = (slot >= 0) & (slot < micro)
        advance_h_buf, advance_dz_buf, advance_dx_buf, advance_gain_acc, advance_conv_acc = buffers
        clipped = jnp.clip(slot, 0, micro - 1)
        dy = jnp.where(rank == sections - 1, top[clipped], incoming)
        dx, h, dz, dgain, dconv = layer_backward(
            saved[clipped], dy, masks[clipped], kernel, gain, proj
        )
        advance_h_buf = advance_h_buf.at[clipped].set(jnp.where(active, h, advance_h_buf[clipped]))
        advance_dz_buf = advance_dz_buf.at[clipped].set(
            jnp.where(active, dz, advance_dz_buf[clipped])
        )
        advance_dx_buf = advance_dx_buf.at[clipped].set(
            jnp.where(active, dx, advance_dx_buf[clipped])
        )
        advance_gain_acc = advance_gain_acc + jnp.where(active, dgain, 0.0)
        advance_conv_acc = advance_conv_acc + jnp.where(active, dconv, 0.0)
        dx, buffers = (
            dx,
            (advance_h_buf, advance_dz_buf, advance_dx_buf, advance_gain_acc, advance_conv_acc),
        )
        if tick + 1 < ticks:
            incoming = from_behind(dx, "section", -1)
    h_buf, dz_buf, dx_buf, gain_acc, conv_acc = buffers
    h_all = h_buf.reshape(rows, width)
    dz_all = dz_buf.reshape(rows, width)
    scale = 1.0 / groups
    local = lax.dot_general(
        h_all, dz_all, (((0,), (0,)), ((), ())), preferred_element_type=jnp.float32
    )
    proj_grad, conv_grad, gain_grad = (
        lax.psum_scatter(local, "dp", scatter_dimension=0, tiled=True),
        lax.psum_scatter(conv_acc, "dp", scatter_dimension=1, tiled=True),
        lax.psum_scatter(gain_acc, "dp", scatter_dimension=0, tiled=True),
    )
    section_grads = dx_buf.reshape(rows, width)[None]
    return (
        section_grads,
        (proj_grad * scale)[None],
        (conv_grad * scale)[None],
        (gain_grad * scale)[None],
    )


def solution(mesh):
    return jax.shard_map(
        body,
        mesh=mesh,
        in_specs=(
            P("dp", None),
            P("section", "dp", None),
            P(),
            P("dp"),
            P("section", None, None),
            P("section", None),
            P("section", None, None),
        ),
        out_specs=(
            P("section", "dp", None),
            P("section", "dp", None),
            P("section", None, "dp"),
            P("section", "dp"),
        ),
        check_vma=False,
    )
```

profile of v0, /device:TPU:8, one launch (start us, length us, event | category | flops | bytes accessed | tf_op | source)
XLA Modules:
  0.0 647.9 jit_solution(16357194788171526564)
XLA Ops:
  11.3 1.4 convert_multiply_fusion.8
  14.6 4.6 multiply_reduce_fusion.6
  22.3 2.3 bitcast_dynamic-update-slice_fusion.1
  24.7 4.3 collective-permute-start
  38.1 1.8 fusion.538
  41.1 1.5 bitcast_dynamic-update-slice_fusion
  43.5 1.5 and_reduce_fusion
  45.0 1.5 fusion.501
  47.4 1.5 fusion.500
  49.8 2.2 fusion.499
  52.9 1.5 fusion.498
  55.3 2.1 fusion.497
  57.4 1.6 constant_dynamic-slice_fusion.6
  98.7 2.5 fusion.495
  101.3 1.6 constant_dynamic-slice_fusion.4
  103.1 4.5 multiply_reduce_fusion.5
  119.2 3.3 fusion.507
  130.9 2.4 collective-permute-start.1
  135.3 1.5 fusion.496
  136.8 5.9 stack.735
  144.0 2.5 fusion.494
  147.5 4.6 multiply_reduce_fusion.4
  153.7 2.3 fusion.506
  173.9 1.9 collective-permute-start.2
  176.7 4.2 collective-permute-done.2
  181.7 2.8 multiply_reduce_fusion.3
  185.9 2.3 fusion.505
  206.1 2.1 collective-permute-start.3
  209.1 4.0 collective-permute-done.3
  213.9 2.1 multiply_reduce_fusion.2
  217.4 2.3 fusion.504
  237.5 1.9 collective-permute-start.4
  240.4 4.2 collective-permute-done.4
  245.3 2.1 multiply_reduce_fusion.1
  248.7 2.2 fusion.503
  268.8 2.1 collective-permute-start.5
  271.0 4.9 collective-permute-done.5
  276.9 1.6 multiply_reduce_fusion
  282.1 3.5 stack.863
  285.6 3.5 stack.831
  289.1 3.5 stack.799
  292.6 3.5 stack.767
  297.3 6.3 convolution_bitcast_fusion
  306.5 127.5 %all-reduce.15 = f32[1536]{0:T(1024)S(1)} all-reduce(f32[1536]{0:T(1024)S(1)} %select_add_fusion.1), channel_id=4, replica_groups=mesh['section'=4,'dp'=64] {'dp'}, use_global_device_ids=true, to_apply=%region_262.263.clone | all-reduce | flops 1536 | bytes 12288
  434.9 2.3 fusion.502
  437.1 43.4 %all-reduce.18.cloned.1.call-done = f32[31,1536]{1,0:T(8,128)} async-done(((f32[31,1536]{1,0:T(8,128)}), f32[31,1536]{1,0:T(8,128)}) %all-reduce.18.cloned.1.call-update) | async-done | bytes 190480
  482.0 157.3 %reduce-scatter.3.cloned.1.call-done = f32[24,1536]{1,0:T(8,128)} async-done(((f32[1536,1536]{1,0:T(8,128)}), f32[24,1536]{1,0:T(8,128)}) %reduce-scatter.3.cloned.1.call-update) | async-done | bytes 147472 | tf_op jit(solution)/shard_map/reduce_scatter | solution.py:110
  639.3 1.6 multiply_bitcast_fusion
  (746 shorter events, 177.4 us)
Async XLA Ops:
  7.2 473.3 %all-reduce.18.cloned.1.call-start = ((), (), s32[]{:S(2)}) async-start(), calls=%async_computation.2 | async-start | bytes 393216
  24.7 74.1 %collective-permute-start = (bf16[48,1536]{1,0:T(8,128)(2,1)}, bf16[48,1536]{1,0:T(8,128)(2,1)}, u32[]{:S(2)}, u32[]{:S(2)}) collective-permute-start(bf16[48,1536]{1,0:T(8,128)(2,1)} %get-tuple-element.585), channel_id=1, source_target_pairs={{64,0},{128,64},{192,128},{65,1},{129,65},{193,129},{66,2},{130,66... | collective-permute-start | bytes 442376 | tf_op jit(solution)/shard_map/ppermute | solution.py:12
  37.9 59.9 %copy-start.192 = (f32[48]{0:T(128)}, f32[48]{0:T(128)S(1)}, u32[]{:S(2)}) copy-start(f32[48]{0:T(128)S(1)} %broadcast_multiply_fusion.14) | copy-start | bytes 580
  38.1 59.6 %copy-start.204 = (f32[48]{0:T(128)}, f32[48]{0:T(128)S(1)}, u32[]{:S(2)}) copy-start(f32[48]{0:T(128)S(1)} %add_rsqrt_fusion.4) | copy-start | bytes 580
  40.0 57.7 %copy-start.194 = (f32[48]{0:T(128)}, f32[48]{0:T(128)S(1)}, u32[]{:S(2)}) copy-start(f32[48]{0:T(128)S(1)} %broadcast_multiply_fusion.17) | copy-start | bytes 580
  40.2 57.5 %copy-start.206 = (f32[48]{0:T(128)}, f32[48]{0:T(128)S(1)}, u32[]{:S(2)}) copy-start(f32[48]{0:T(128)S(1)} %add_rsqrt_fusion.5) | copy-start | bytes 580
  130.9 13.1 %collective-permute-start.1 = (bf16[48,1536]{1,0:T(8,128)(2,1)}, bf16[48,1536]{1,0:T(8,128)(2,1)}, u32[]{:S(2)}, u32[]{:S(2)}) collective-permute-start(bf16[48,1536]{1,0:T(8,128)(2,1)} %get-tuple-element.581), channel_id=1, source_target_pairs={{64,0},{128,64},{192,128},{65,1},{129,65},{193,129},{66,2},{130,66... | collective-permute-start | bytes 442376 | tf_op jit(solution)/shard_map/ppermute | solution.py:12
  147.4 34.3 %slice-start = ((s8[4718592]{0:T(1024)(128)(4,1)}), s8[4194304]{0:T(1024)(128)(4,1)S(1)}, s32[]{:S(2)}) async-start(s8[4718592]{0:T(1024)(128)(4,1)} %bitcast.293), calls=%async_computation.3 | async-start | bytes 8388608
  147.4 33.5 %copy-start.6 = (bf16[4,48,1536]{2,1,0:T(8,128)(2,1)S(1)}, bf16[4,48,1536]{2,1,0:T(8,128)(2,1)}, u32[]{:S(2)}) copy-start(bf16[4,48,1536]{2,1,0:T(8,128)(2,1)} %get-tuple-element.558) | copy-start | bytes 1769476
  147.4 33.5 %copy-start.9 = (bf16[192,1536]{1,0:T(8,128)(2,1)S(1)}, bf16[192,1536]{1,0:T(8,128)(2,1)}, u32[]{:S(2)}) copy-start(bf16[192,1536]{1,0:T(8,128)(2,1)} %param.49) | copy-start | bytes 1769476
  147.4 33.5 %copy-start.176 = (f32[48]{0:T(128)S(1)}, f32[48]{0:T(128)}, u32[]{:S(2)}) copy-start(f32[48]{0:T(128)} %copy-done.175) | copy-start | bytes 580
  147.5 34.2 %slice-start.1 = ((s8[4718592]{0:T(1024)(128)(4,1)}), s8[524288]{0:T(1024)(128)(4,1)S(1)}, s32[]{:S(2)}) async-start(s8[4718592]{0:T(1024)(128)(4,1)} %bitcast.293), calls=%async_computation.4 | async-start | bytes 1048576
  173.9 7.0 %collective-permute-start.2 = (bf16[48,1536]{1,0:T(8,128)(2,1)S(1)}, bf16[48,1536]{1,0:T(8,128)(2,1)S(1)}, u32[]{:S(2)}, u32[]{:S(2)}) collective-permute-start(bf16[48,1536]{1,0:T(8,128)(2,1)S(1)} %get-tuple-element.577), channel_id=1, source_target_pairs={{64,0},{128,64},{192,128},{65,1},{129,65},{193,129},{66,2},{130,66... | collective-permute-start | bytes 442376 | tf_op jit(solution)/shard_map/ppermute | solution.py:12
  206.1 7.0 %collective-permute-start.3 = (bf16[48,1536]{1,0:T(8,128)(2,1)S(1)}, bf16[48,1536]{1,0:T(8,128)(2,1)S(1)}, u32[]{:S(2)}, u32[]{:S(2)}) collective-permute-start(bf16[48,1536]{1,0:T(8,128)(2,1)S(1)} %get-tuple-element.573), channel_id=1, source_target_pairs={{64,0},{128,64},{192,128},{65,1},{129,65},{193,129},{66,2},{130,66... | collective-permute-start | bytes 442376 | tf_op jit(solution)/shard_map/ppermute | solution.py:12
  237.5 7.0 %collective-permute-start.4 = (bf16[48,1536]{1,0:T(8,128)(2,1)S(1)}, bf16[48,1536]{1,0:T(8,128)(2,1)S(1)}, u32[]{:S(2)}, u32[]{:S(2)}) collective-permute-start(bf16[48,1536]{1,0:T(8,128)(2,1)S(1)} %get-tuple-element.569), channel_id=1, source_target_pairs={{64,0},{128,64},{192,128},{65,1},{129,65},{193,129},{66,2},{130,66... | collective-permute-start | bytes 442376 | tf_op jit(solution)/shard_map/ppermute | solution.py:12
  268.8 7.0 %collective-permute-start.5 = (bf16[48,1536]{1,0:T(8,128)(2,1)S(1)}, bf16[48,1536]{1,0:T(8,128)(2,1)S(1)}, u32[]{:S(2)}, u32[]{:S(2)}) collective-permute-start(bf16[48,1536]{1,0:T(8,128)(2,1)S(1)} %get-tuple-element.565), channel_id=1, source_target_pairs={{64,0},{128,64},{192,128},{65,1},{129,65},{193,129},{66,2},{130,66... | collective-permute-start | bytes 442376 | tf_op jit(solution)/shard_map/ppermute | solution.py:12
  297.2 342.0 %reduce-scatter.3.cloned.1.call-start = ((), (), s32[]{:S(2)}) async-start(), calls=%async_computation.1 | async-start | bytes 9584640 | tf_op jit(solution)/shard_map/reduce_scatter | solution.py:110
  303.6 131.0 %copy-start.13 = (f32[1536]{0:T(1024)S(1)}, f32[1536]{0:T(1024)}, u32[]{:S(2)}) copy-start(f32[1536]{0:T(1024)} %copy-done.10) | copy-start | bytes 18436
  303.6 131.0 %copy-start.17 = (f32[1536]{0:T(1024)S(1)}, f32[1536]{0:T(1024)}, u32[]{:S(2)}) copy-start(f32[1536]{0:T(1024)} %copy-done.14) | copy-start | bytes 18436
  303.6 131.0 %copy-start.21 = (f32[1536]{0:T(1024)S(1)}, f32[1536]{0:T(1024)}, u32[]{:S(2)}) copy-start(f32[1536]{0:T(1024)} %copy-done.18) | copy-start | bytes 18436
  303.6 131.0 %copy-start.25 = (f32[1536]{0:T(1024)S(1)}, f32[1536]{0:T(1024)}, u32[]{:S(2)}) copy-start(f32[1536]{0:T(1024)} %copy-done.22) | copy-start | bytes 18436
  303.7 130.9 %copy-start.29 = (f32[1536]{0:T(1024)S(1)}, f32[1536]{0:T(1024)}, u32[]{:S(2)}) copy-start(f32[1536]{0:T(1024)} %copy-done.26) | copy-start | bytes 18436
  303.7 130.9 %copy-start.33 = (f32[1536]{0:T(1024)S(1)}, f32[1536]{0:T(1024)}, u32[]{:S(2)}) copy-start(f32[1536]{0:T(1024)} %copy-done.30) | copy-start | bytes 18436
  303.7 130.9 %copy-start.37 = (f32[1536]{0:T(1024)S(1)}, f32[1536]{0:T(1024)}, u32[]{:S(2)}) copy-start(f32[1536]{0:T(1024)} %copy-done.34) | copy-start | bytes 18436
  303.7 130.9 %copy-start.41 = (f32[1536]{0:T(1024)S(1)}, f32[1536]{0:T(1024)}, u32[]{:S(2)}) copy-start(f32[1536]{0:T(1024)} %copy-done.38) | copy-start | bytes 18436
  303.7 130.9 %copy-start.45 = (f32[1536]{0:T(1024)S(1)}, f32[1536]{0:T(1024)}, u32[]{:S(2)}) copy-start(f32[1536]{0:T(1024)} %copy-done.42) | copy-start | bytes 18436
  303.7 130.9 %copy-start.49 = (f32[1536]{0:T(1024)S(1)}, f32[1536]{0:T(1024)}, u32[]{:S(2)}) copy-start(f32[1536]{0:T(1024)} %copy-done.46) | copy-start | bytes 18436
  303.7 130.9 %copy-start.53 = (f32[1536]{0:T(1024)S(1)}, f32[1536]{0:T(1024)}, u32[]{:S(2)}) copy-start(f32[1536]{0:T(1024)} %copy-done.50) | copy-start | bytes 18436
  303.7 130.9 %copy-start.57 = (f32[1536]{0:T(1024)S(1)}, f32[1536]{0:T(1024)}, u32[]{:S(2)}) copy-start(f32[1536]{0:T(1024)} %copy-done.54) | copy-start | bytes 18436
  303.7 130.9 %copy-start.61 = (f32[1536]{0:T(1024)S(1)}, f32[1536]{0:T(1024)}, u32[]{:S(2)}) copy-start(f32[1536]{0:T(1024)} %copy-done.58) | copy-start | bytes 18436
  303.7 130.9 %copy-start.65 = (f32[1536]{0:T(1024)S(1)}, f32[1536]{0:T(1024)}, u32[]{:S(2)}) copy-start(f32[1536]{0:T(1024)} %copy-done.62) | copy-start | bytes 18436
  303.8 130.9 %copy-start.69 = (f32[1536]{0:T(1024)S(1)}, f32[1536]{0:T(1024)}, u32[]{:S(2)}) copy-start(f32[1536]{0:T(1024)} %copy-done.66) | copy-start | bytes 18436
  303.8 130.9 %copy-start.73 = (f32[1536]{0:T(1024)S(1)}, f32[1536]{0:T(1024)}, u32[]{:S(2)}) copy-start(f32[1536]{0:T(1024)} %copy-done.70) | copy-start | bytes 18436
  303.8 130.9 %copy-start.77 = (f32[1536]{0:T(1024)S(1)}, f32[1536]{0:T(1024)}, u32[]{:S(2)}) copy-start(f32[1536]{0:T(1024)} %copy-done.74) | copy-start | bytes 18436
  303.8 130.9 %copy-start.81 = (f32[1536]{0:T(1024)S(1)}, f32[1536]{0:T(1024)}, u32[]{:S(2)}) copy-start(f32[1536]{0:T(1024)} %copy-done.78) | copy-start | bytes 18436
  303.8 130.9 %copy-start.85 = (f32[1536]{0:T(1024)S(1)}, f32[1536]{0:T(1024)}, u32[]{:S(2)}) copy-start(f32[1536]{0:T(1024)} %copy-done.82) | copy-start | bytes 18436
  303.8 130.9 %copy-start.89 = (f32[1536]{0:T(1024)S(1)}, f32[1536]{0:T(1024)}, u32[]{:S(2)}) copy-start(f32[1536]{0:T(1024)} %copy-done.86) | copy-start | bytes 18436
  303.8 130.9 %copy-start.93 = (f32[1536]{0:T(1024)S(1)}, f32[1536]{0:T(1024)}, u32[]{:S(2)}) copy-start(f32[1536]{0:T(1024)} %copy-done.90) | copy-start | bytes 18436
  303.8 130.9 %copy-start.97 = (f32[1536]{0:T(1024)S(1)}, f32[1536]{0:T(1024)}, u32[]{:S(2)}) copy-start(f32[1536]{0:T(1024)} %copy-done.94) | copy-start | bytes 18436
  303.8 130.9 %copy-start.101 = (f32[1536]{0:T(1024)S(1)}, f32[1536]{0:T(1024)}, u32[]{:S(2)}) copy-start(f32[1536]{0:T(1024)} %copy-done.98) | copy-start | bytes 18436
  303.8 130.9 %copy-start.105 = (f32[1536]{0:T(1024)S(1)}, f32[1536]{0:T(1024)}, u32[]{:S(2)}) copy-start(f32[1536]{0:T(1024)} %copy-done.102) | copy-start | bytes 18436
  303.9 130.9 %copy-start.109 = (f32[1536]{0:T(1024)S(1)}, f32[1536]{0:T(1024)}, u32[]{:S(2)}) copy-start(f32[1536]{0:T(1024)} %copy-done.106) | copy-start | bytes 18436
  303.9 130.9 %copy-start.113 = (f32[1536]{0:T(1024)S(1)}, f32[1536]{0:T(1024)}, u32[]{:S(2)}) copy-start(f32[1536]{0:T(1024)} %copy-done.110) | copy-start | bytes 18436
  303.9 130.9 %copy-start.117 = (f32[1536]{0:T(1024)S(1)}, f32[1536]{0:T(1024)}, u32[]{:S(2)}) copy-start(f32[1536]{0:T(1024)} %copy-done.114) | copy-start | bytes 18436
  303.9 130.9 %copy-start.121 = (f32[1536]{0:T(1024)S(1)}, f32[1536]{0:T(1024)}, u32[]{:S(2)}) copy-start(f32[1536]{0:T(1024)} %copy-done.118) | copy-start | bytes 18436
  303.9 130.9 %copy-start.125 = (f32[1536]{0:T(1024)S(1)}, f32[1536]{0:T(1024)}, u32[]{:S(2)}) copy-start(f32[1536]{0:T(1024)} %copy-done.122) | copy-start | bytes 18436
  303.9 130.9 %copy-start.129 = (f32[1536]{0:T(1024)S(1)}, f32[1536]{0:T(1024)}, u32[]{:S(2)}) copy-start(f32[1536]{0:T(1024)} %copy-done.126) | copy-start | bytes 18436
  303.9 130.9 %copy-start.168 = (f32[48]{0:T(128)S(1)}, f32[48]{0:T(128)}, u32[]{:S(2)}) copy-start(f32[48]{0:T(128)} %get-tuple-element.595) | copy-start | bytes 580
  (174 other events, 3012.7 us)
Sparse Core Ops, SparseCore 0:
  297.4 183.0 all-reduce.17
  484.8 154.4 reduce-scatter.2
where the time goes:
time: 656 us; the launch traced here: 648 us
  waiting for transfers between devices  218 us (33%)
  local copies, waits for them, and re-layouts  173 us (26%)
  blocking collectives  127 us (19%)
  other arithmetic  67.4 us (10%)
  matrix products  28.7 us (4%)
  between operations  18.7 us (3%)
  starting transfers between devices  14.9 us (2%)
    reduce_scatter x1, waiting for transfers between devices, body(): lax.psum_scatter(local, 'dp', scatter_dimension=0, tiled=True)  157 us
    another operation x224, local copies, waits for them, and re-layouts, layer_backward(): jnp.stack([jnp.sum(da * upad[j:j + frames], axis=0) for j in range(taps)])  150 us
    unnamed x1, blocking collectives  127 us
    unnamed x3, waiting for transfers between devices  43.4 us
    dot_general x7, matrix products, layer_backward(): lax.dot_general(dz, proj, (((1,), (1,)), ((), ())), preferred_element_typ...  22.4 us
    ppermute x6, waiting for transfers between devices, from_behind(): return lax.ppermute(value, axis, pairs)  17.2 us
    scatter x7, other arithmetic, body(): advance_dx_buf.at[clipped]  16.9 us
    ppermute x6, starting transfers between devices, from_behind(): return lax.ppermute(value, axis, pairs)  14.8 us
  transfers between devices with their start and end apart: 8, of which 6 were waited for; matrix products, arithmetic and copies ran while one was open for 14% of the time, Pallas kernels for 0%

commit v1 on v0

v1 whole, which is shorter than its diff:
```python
import jax
import jax.numpy as jnp
from jax import lax
from jax.sharding import PartitionSpec as P

eps = 1e-05


def from_behind(value, axis, by):
    size = lax.axis_size(axis)
    pairs = [(i, i + by) for i in range(size) if 0 <= i + by < size]
    return lax.ppermute(value, axis, pairs)


def layer_forward(x, mask, kernel):
    taps = kernel.shape[0]
    half = (taps - 1) // 2
    frames = x.shape[1]
    u = x.astype(jnp.float32) * mask
    upad = jnp.pad(u, ((0, 0), (half, half), (0, 0)))
    a = jnp.zeros(u.shape, jnp.float32)
    for j in range(taps):
        a = a + kernel[j] * upad[:, j : j + frames]
    return upad, a


def norm_forward(a, gain):
    mean = jnp.mean(a, axis=-1, keepdims=True)
    cen = a - mean
    var = jnp.mean(cen * cen, axis=-1, keepdims=True)
    inv = lax.rsqrt(var + eps)
    nhat = cen * inv
    n = nhat * gain
    sig = jax.nn.sigmoid(n)
    h = (n * sig).astype(jnp.bfloat16)
    slope = sig + n * sig * (1.0 - sig)
    return inv, nhat, h, slope


def layer_backward(dy, mask, kernel, gain, proj, inv, nhat, slope):
    taps = kernel.shape[0]
    half = (taps - 1) // 2
    frames = dy.shape[0]
    dz = (dy.astype(jnp.float32) * mask).astype(jnp.bfloat16)
    dh = lax.dot_general(dz, proj, (((1,), (1,)), ((), ())), preferred_element_type=jnp.float32)
    dn = dh * slope
    dnh = dn * gain
    da = inv * (
        dnh
        - jnp.mean(dnh, axis=-1, keepdims=True)
        - nhat * jnp.mean(dnh * nhat, axis=-1, keepdims=True)
    )
    dapad = jnp.pad(da, ((half, half), (0, 0)))
    du = jnp.zeros(da.shape, jnp.float32)
    for j in range(taps):
        du = du + kernel[j] * dapad[2 * half - j : 2 * half - j + frames]
    dx = (dy.astype(jnp.float32) + mask * du).astype(jnp.bfloat16)
    return dx, dz, dn, da


def body(grad_out, section_inputs, lengths, bucket_list, conv_weight, norm_gain, projection):
    sections = lax.axis_size("section")
    groups = lax.axis_size("dp")
    rank = lax.axis_index("section")
    micro = bucket_list.shape[0]
    rows, width = grad_out.shape
    frames = rows // micro
    table = jnp.arange(lengths.shape[0], dtype=jnp.int32)
    lens = jnp.sum(jnp.where(bucket_list[:, None] == table[None, :], lengths[None, :], 0), axis=1)
    masks = (jnp.arange(frames, dtype=jnp.int32)[None, :] < lens[:, None]).astype(jnp.float32)[
        ..., None
    ]
    saved = section_inputs[0].reshape(micro, frames, width)
    top = grad_out.reshape(micro, frames, width)
    kernel = conv_weight[0]
    gain = norm_gain[0]
    proj = projection[0]
    taps = kernel.shape[0]

    upad, a = layer_forward(saved, masks, kernel)
    inv, nhat, h, slope = norm_forward(a, gain)

    dz_buf = jnp.zeros((micro, frames, width), jnp.bfloat16)
    dx_buf = jnp.zeros((micro, frames, width), jnp.bfloat16)
    dn_buf = jnp.zeros((micro, frames, width), jnp.float32)
    da_buf = jnp.zeros((micro, frames, width), jnp.float32)
    incoming = jnp.zeros((frames, width), jnp.bfloat16)
    ticks = micro + sections - 1
    for tick in range(ticks):
        slot = tick - (sections - 1 - rank)
        active = (slot >= 0) & (slot < micro)
        clipped = jnp.clip(slot, 0, micro - 1)
        dy = jnp.where(rank == sections - 1, top[clipped], incoming)
        dx, dz, dn, da = layer_backward(
            dy, masks[clipped], kernel, gain, proj, inv[clipped], nhat[clipped], slope[clipped]
        )
        dz_buf = dz_buf.at[clipped].set(jnp.where(active, dz, dz_buf[clipped]))
        dx_buf = dx_buf.at[clipped].set(jnp.where(active, dx, dx_buf[clipped]))
        dn_buf = dn_buf.at[clipped].set(jnp.where(active, dn, dn_buf[clipped]))
        da_buf = da_buf.at[clipped].set(jnp.where(active, da, da_buf[clipped]))
        if tick + 1 < ticks:
            incoming = from_behind(dx, "section", -1)

    h_all = h.reshape(rows, width)
    dz_all = dz_buf.reshape(rows, width)
    local = lax.dot_general(
        h_all, dz_all, (((0,), (0,)), ((), ())), preferred_element_type=jnp.float32
    )
    windows = jnp.stack([upad[:, j : j + frames] for j in range(taps)], axis=0)
    conv_acc = jnp.sum(windows * da_buf[None], axis=(1, 2))
    gain_acc = jnp.sum(dn_buf * nhat, axis=(0, 1))

    extra = jnp.concatenate([conv_acc.T, gain_acc[:, None]], axis=1)
    mine_p, mine_e = lax.psum_scatter((local, extra), "dp", scatter_dimension=0, tiled=True)
    mine = jnp.concatenate([mine_p, mine_e], axis=1)
    scale = 1.0 / groups
    proj_grad = mine[:, :width]
    conv_grad = mine[:, width : width + taps].T
    gain_grad = mine[:, width + taps]
    section_grads = dx_buf.reshape(rows, width)[None]
    return (
        section_grads,
        (proj_grad * scale)[None],
        (conv_grad * scale)[None],
        (gain_grad * scale)[None],
    )


def solution(mesh):
    return jax.shard_map(
        body,
        mesh=mesh,
        in_specs=(
            P("dp", None),
            P("section", "dp", None),
            P(),
            P("dp"),
            P("section", None, None),
            P("section", None),
            P("section", None, None),
        ),
        out_specs=(
            P("section", "dp", None),
            P("section", "dp", None),
            P("section", None, "dp"),
            P("section", "dp"),
        ),
        check_vma=False,
    )
```

time: 656 us -> 498 us (0.76); the launches traced: 648 us -> 497 us
  local copies, waits for them, and re-layouts: 173 us -> 25.6 us
  waiting for transfers between devices: 218 us -> 358 us
  blocking collectives: 127 us -> 0 us
  other arithmetic: 67.4 us -> 58.8 us
    another operation x224 -> x5, local copies, waits for them, and re-layouts: 150 us -> 0.43 us  [layer_backward(): jnp.stack([jnp.sum(da * upad[j:j + frames], axis=0) for j in range(taps)])]
    unnamed x3, waiting for transfers between devices: 43.4 us -> 178 us
    unnamed x1 -> x0, blocking collectives: 127 us -> none
    unnamed x430 -> x352, local copies, waits for them, and re-layouts: 3.15 us -> 16.4 us
    scatter x21 -> x22, other arithmetic: 37.2 us -> 26.4 us  [the longest x7 13.1 us: body(): dx_buf = dx_buf.at[clipped].set(jnp.where(active, dx, dx_buf[clipped]))]
    dynamic_slice x17 -> x24, local copies, waits for them, and re-layouts: 15.1 us -> 4.62 us  [the longest x6 1.73 us: body(): dn_buf = dn_buf.at[clipped].set(jnp.where(active, dn, dn_buf[clipped]))]
    ppermute x6, waiting for transfers between devices: 17.2 us -> 24.7 us  [from_behind(): return lax.ppermute(value, axis, pairs)]
    reduce_sum x29 -> x4, other arithmetic: 19.2 us -> 21.1 us  [the longest x1 14.9 us: body(): conv_acc = jnp.sum(windows * da_buf[None], axis=(1, 2))]
  transfers between devices with their start and end apart: 8 -> 8, of which waited for: 6 -> 7; matrix products, arithmetic and copies ran while one was open for 14% -> 4% of each run, Pallas kernels for 0% -> 0%
where the time goes in v1:
time: 498 us; the launch traced here: 497 us
  waiting for transfers between devices  358 us (72%)
  other arithmetic  58.8 us (12%)
  local copies, waits for them, and re-layouts  25.6 us (5%)
  matrix products  22.2 us (4%)
  between operations  17.6 us (4%)
  starting transfers between devices  14.2 us (3%)
    unnamed x3, waiting for transfers between devices  178 us
    reduce_scatter x1, waiting for transfers between devices, body(): lax.psum_scatter((local, extra), 'dp', scatter_dimension=0, tiled=True)  156 us
    ppermute x6, waiting for transfers between devices, from_behind(): return lax.ppermute(value, axis, pairs)  24.7 us
    dot_general x7, matrix products, layer_backward(): lax.dot_general(dz, proj, (((1,), (1,)), ((), ())), preferred_element_typ...  17 us
    unnamed x352, local copies, waits for them, and re-layouts  16.4 us
    reduce_sum x1, other arithmetic, body(): conv_acc = jnp.sum(windows * da_buf[None], axis=(1, 2))  14.9 us
    ppermute x6, starting transfers between devices, from_behind(): return lax.ppermute(value, axis, pairs)  14.1 us
    scatter x7, other arithmetic, body(): dx_buf = dx_buf.at[clipped].set(jnp.where(active, dx, dx_buf[clipped]))  13.1 us
  transfers between devices with their start and end apart: 8, of which 7 were waited for; matrix products, arithmetic and copies ran while one was open for 4% of the time, Pallas kernels for 0%

profile of v1, /device:TPU:8, one launch (start us, length us, event | category | flops | bytes accessed | tf_op | source)
XLA Modules:
  0.0 496.7 jit_solution(12252469423998506632)
XLA Ops:
  7.2 1.2 slice_reduce_fusion.30
  8.6 1.0 slice_reduce_fusion.29
  9.7 0.9 select_reduce_fusion
  10.7 1.2 convert_element_type.150
  12.1 0.9 copy-done.3
  13.2 5.7 %fusion.567 = (f32[4,48]{1,0:T(4,128)S(1)}, f32[4,48,1536]{2,1,0:T(8,128)S(1)}) fusion(f32[1536]{0:T(1024)S(1)} %get-tuple-element.383, f32[1536]{0:T(1024)S(1)} %get-tuple-element.384, f32[1536]{0:T(1024)S(1)} %get-tuple-element.355, f32[1536]{0:T(1024)S(1)} %get-tuple-element.356, f32[1536]{0:T(1024)S(1)} %get-tuple-element.357, ...), kind=kLoop, calls=%fused_computation.1020 | loop fusion | flops 18284352 | bytes 2550528 | tf_op jit(solution)/shard_map/reduce_sum | solution.py:28
  19.8 1.3 multiply_add_fusion
  22.2 4.8 multiply_reduce_fusion.9
  29.3 1.5 bitcast_dynamic-update-slice_fusion.31
  31.2 2.3 bitcast_dynamic-update-slice_fusion.32
  33.5 4.2 collective-permute-start
  39.5 1.1 copy-done.4
  43.5 1.1 constant_dynamic-slice_fusion.17
  45.5 1.6 constant_dynamic-slice_fusion.5
  47.1 7.8 %copy-done = f32[31,4,48,1536]{3,2,1,0:T(8,128)} copy-done((f32[31,4,48,1536]{3,2,1,0:T(8,128)}, f32[31,4,48,1536]{3,2,1,0:T(8,128)S(1)}, u32[]{:S(2)}) %copy-start) | copy-done | bytes 36569112
  56.7 0.8 and_reduce_fusion
  57.5 1.9 fusion.519
  60.3 4.1 multiply_reduce_fusion.8
  64.8 0.9 fusion.492
  66.0 2.7 fusion.525
  68.7 1.9 collective-permute-start.1
  70.8 5.0 collective-permute-done.1
  76.6 1.6 multiply_reduce_fusion.7
  79.0 1.6 fusion.524
  80.6 1.9 collective-permute-start.2
  82.7 5.0 %collective-permute-done.2 = bf16[48,1536]{1,0:T(8,128)(2,1)S(1)} collective-permute-done((bf16[48,1536]{1,0:T(8,128)(2,1)S(1)}, bf16[48,1536]{1,0:T(8,128)(2,1)S(1)}, u32[]{:S(2)}, u32[]{:S(2)}) %collective-permute-start.2) | collective-permute-done | bytes 147488 | tf_op jit(solution)/shard_map/ppermute | solution.py:12
  88.4 1.6 multiply_reduce_fusion.6
  90.8 1.6 fusion.523
  92.4 2.1 collective-permute-start.3
  94.7 4.8 collective-permute-done.3
  100.2 1.6 multiply_reduce_fusion.5
  102.7 1.6 fusion.522
  104.3 1.9 collective-permute-start.4
  106.4 5.0 %collective-permute-done.4 = bf16[48,1536]{1,0:T(8,128)(2,1)S(1)} collective-permute-done((bf16[48,1536]{1,0:T(8,128)(2,1)S(1)}, bf16[48,1536]{1,0:T(8,128)(2,1)S(1)}, u32[]{:S(2)}, u32[]{:S(2)}) %collective-permute-start.4) | collective-permute-done | bytes 147488 | tf_op jit(solution)/shard_map/ppermute | solution.py:12
  112.1 1.6 multiply_reduce_fusion.4
  114.6 1.6 fusion.521
  116.2 1.9 collective-permute-start.5
  118.2 5.0 %collective-permute-done.5 = bf16[48,1536]{1,0:T(8,128)(2,1)S(1)} collective-permute-done((bf16[48,1536]{1,0:T(8,128)(2,1)S(1)}, bf16[48,1536]{1,0:T(8,128)(2,1)S(1)}, u32[]{:S(2)}, u32[]{:S(2)}) %collective-permute-start.5) | collective-permute-done | bytes 147488 | tf_op jit(solution)/shard_map/ppermute | solution.py:12
  124.1 1.6 multiply_reduce_fusion.3
  126.7 14.9 %multiply_reduce_fusion = f32[31,1536]{1,0:T(8,128)S(1)} fusion(f32[31,4,48,1536]{3,2,1,0:T(8,128)} %copy-done, f32[4,48,1536]{2,1,0:T(8,128)S(1)} %get-tuple-element.391), kind=kLoop, calls=%fused_computation | loop fusion | flops 18236928 | bytes 37939200 | tf_op jit(solution)/shard_map/reduce_sum | solution.py:110
  141.7 1.2 copy.13
  142.9 5.1 %convolution_bitcast_fusion = f32[1536,1536]{1,0:T(8,128)} fusion(bf16[4,48,1536]{2,1,0:T(8,128)(2,1)S(1)} %copy-done.13, f32[4,48,1536]{2,1,0:T(8,128)S(1)} %get-tuple-element.430, f32[1536]{0:T(1024)S(1)} %reduce.122), kind=kOutput, calls=%fused_computation.31 | convolution fusion | flops 907739136 | bytes 11212800 | tf_op jit(solution)/shard_map/dot_general | solution.py:106
  150.3 1.7 fusion.520
  151.9 177.8 %all-reduce.11.cloned.1.call-done = f32[1536,32]{1,0:T(8,128)} async-done(((f32[1536,32]{1,0:T(8,128)}), f32[1536,32]{1,0:T(8,128)}) %all-reduce.11.cloned.1.call-update) | async-done | bytes 196624
  329.7 1.4 fusion.535
  331.1 1.3 fusion.536
  332.4 155.8 %reduce-scatter.2.cloned.1.call-done = f32[24,1536]{1,0:T(8,128)} async-done(((f32[1536,1536]{1,0:T(8,128)}), f32[24,1536]{1,0:T(8,128)}) %reduce-scatter.2.cloned.1.call-update) | async-done | bytes 147472 | tf_op jit(solution)/shard_map/reduce_scatter | solution.py:114
  488.3 1.6 multiply_bitcast_fusion
  (420 shorter events, 22.1 us)
Async XLA Ops:
  7.2 322.6 %all-reduce.11.cloned.1.call-start = ((), (), s32[]{:S(2)}) async-start(), calls=%async_computation.2 | async-start | bytes 1572864
  8.4 4.5 copy-start.21
  8.4 4.5 copy-start.24
  8.4 4.5 copy-start.27
  8.4 4.5 copy-start.30
  8.4 4.5 copy-start.33
  8.4 4.5 copy-start.36
  8.5 4.5 copy-start.39
  8.5 4.5 copy-start.42
  8.5 4.5 copy-start.45
  8.5 4.5 copy-start.49
  8.5 4.5 copy-start.53
  8.5 4.5 copy-start.57
  8.5 4.5 copy-start.61
  8.5 4.5 copy-start.65
  8.5 4.5 copy-start.69
  8.5 4.5 copy-start.73
  8.6 4.5 copy-start.77
  8.6 4.5 copy-start.81
  21.9 5.1 %copy-start.138 = (f32[48]{0:T(128)}, f32[48]{0:T(128)S(1)}, u32[]{:S(2)}) copy-start(f32[48]{0:T(128)S(1)} %get-tuple-element.452) | copy-start | bytes 580
  22.2 5.8 %copy-start.154 = (s32[3]{0:T(128)S(1)}, s32[3]{0:T(128)}, u32[]{:S(2)}) copy-start(s32[3]{0:T(128)} %constant.611.clone.1) | copy-start | bytes 40
  33.5 22.6 %copy-start.7 = (bf16[4,48,1536]{2,1,0:T(8,128)(2,1)}, bf16[4,48,1536]{2,1,0:T(8,128)(2,1)S(1)}, u32[]{:S(2)}) copy-start(bf16[4,48,1536]{2,1,0:T(8,128)(2,1)S(1)} %get-tuple-element.427) | copy-start | bytes 1769476
  33.5 24.1 %collective-permute-start = (bf16[48,1536]{1,0:T(8,128)(2,1)}, bf16[48,1536]{1,0:T(8,128)(2,1)}, u32[]{:S(2)}, u32[]{:S(2)}) collective-permute-start(bf16[48,1536]{1,0:T(8,128)(2,1)} %get-tuple-element.428), channel_id=1, source_target_pairs={{64,0},{128,64},{192,128},{65,1},{129,65},{193,129},{66,2},{130,66... | collective-permute-start | bytes 442376 | tf_op jit(solution)/shard_map/ppermute | solution.py:12
  42.7 12.2 %copy-start = (f32[31,4,48,1536]{3,2,1,0:T(8,128)}, f32[31,4,48,1536]{3,2,1,0:T(8,128)S(1)}, u32[]{:S(2)}) copy-start(f32[31,4,48,1536]{3,2,1,0:T(8,128)S(1)} %bitcast_dynamic-update-slice_fusion) | copy-start | bytes 109707264
  44.8 11.9 %copy-start.155 = (s32[3]{0:T(128)S(1)}, s32[3]{0:T(128)}, u32[]{:S(2)}) copy-start(s32[3]{0:T(128)} %constant.611.clone.1) | copy-start | bytes 40
  44.8 12.8 %copy-start.146 = (f32[48]{0:T(128)S(1)}, f32[48]{0:T(128)}, u32[]{:S(2)}) copy-start(f32[48]{0:T(128)} %get-tuple-element.451) | copy-start | bytes 580
  45.5 9.8 %copy-start.1 = (f32[4,48,1536]{2,1,0:T(8,128)}, f32[4,48,1536]{2,1,0:T(8,128)S(1)}, u32[]{:S(2)}) copy-start(f32[4,48,1536]{2,1,0:T(8,128)S(1)} %bitcast_dynamic-update-slice_fusion.30) | copy-start | bytes 3538948
  55.3 21.2 %slice-start = ((s8[4718592]{0:T(1024)(128)(4,1)}), s8[524288]{0:T(1024)(128)(4,1)S(1)}, s32[]{:S(2)}) async-start(s8[4718592]{0:T(1024)(128)(4,1)} %bitcast.466), calls=%async_computation.3 | async-start | bytes 1048576
  57.5 7.2 %copy-start.20 = (f32[1,48,1536]{2,1,0:T(8,128)S(1)}, f32[1,48,1536]{2,1,0:T(8,128)}, u32[]{:S(2)}) copy-start(f32[1,48,1536]{2,1,0:T(8,128)} %constant_dynamic-slice_fusion.11) | copy-start | bytes 884740
  60.3 4.5 copy-start.2
  60.3 4.5 copy-start.19
  60.3 4.5 copy-start.153
  60.3 16.3 %slice-start.1 = ((s8[4718592]{0:T(1024)(128)(4,1)}), s8[4194304]{0:T(1024)(128)(4,1)S(1)}, s32[]{:S(2)}) async-start(s8[4718592]{0:T(1024)(128)(4,1)} %bitcast.466), calls=%async_computation.4 | async-start | bytes 8388608
  64.8 5.8 %copy-start.11 = (bf16[4,48,1536]{2,1,0:T(8,128)(2,1)S(1)}, bf16[4,48,1536]{2,1,0:T(8,128)(2,1)}, u32[]{:S(2)}) copy-start(bf16[4,48,1536]{2,1,0:T(8,128)(2,1)} %copy-done.10) | copy-start | bytes 1769476
  66.0 9.7 %copy-start.15 = (bf16[192,1536]{1,0:T(8,128)(2,1)S(1)}, bf16[192,1536]{1,0:T(8,128)(2,1)}, u32[]{:S(2)}) copy-start(bf16[192,1536]{1,0:T(8,128)(2,1)} %param.63) | copy-start | bytes 1769476
  66.0 9.7 %copy-start.145 = (f32[48]{0:T(128)S(1)}, f32[48]{0:T(128)}, u32[]{:S(2)}) copy-start(f32[48]{0:T(128)} %get-tuple-element.450) | copy-start | bytes 580
  68.7 7.0 %collective-permute-start.1 = (bf16[48,1536]{1,0:T(8,128)(2,1)S(1)}, bf16[48,1536]{1,0:T(8,128)(2,1)S(1)}, u32[]{:S(2)}, u32[]{:S(2)}) collective-permute-start(bf16[48,1536]{1,0:T(8,128)(2,1)S(1)} %get-tuple-element.426), channel_id=1, source_target_pairs={{64,0},{128,64},{192,128},{65,1},{129,65},{193,129},{66,2},{130,66... | collective-permute-start | bytes 442376 | tf_op jit(solution)/shard_map/ppermute | solution.py:12
  70.7 5.8 %copy-start.6 = (f32[4,48,1536]{2,1,0:T(8,128)S(1)}, f32[4,48,1536]{2,1,0:T(8,128)}, u32[]{:S(2)}) copy-start(f32[4,48,1536]{2,1,0:T(8,128)} %copy-done.5) | copy-start | bytes 3538948
  79.0 8.7 %copy-start.144 = (f32[48]{0:T(128)S(1)}, f32[48]{0:T(128)}, u32[]{:S(2)}) copy-start(f32[48]{0:T(128)} %get-tuple-element.449) | copy-start | bytes 580
  80.6 7.0 %collective-permute-start.2 = (bf16[48,1536]{1,0:T(8,128)(2,1)S(1)}, bf16[48,1536]{1,0:T(8,128)(2,1)S(1)}, u32[]{:S(2)}, u32[]{:S(2)}) collective-permute-start(bf16[48,1536]{1,0:T(8,128)(2,1)S(1)} %get-tuple-element.424), channel_id=1, source_target_pairs={{64,0},{128,64},{192,128},{65,1},{129,65},{193,129},{66,2},{130,66... | collective-permute-start | bytes 442376 | tf_op jit(solution)/shard_map/ppermute | solution.py:12
  90.8 8.7 %copy-start.143 = (f32[48]{0:T(128)S(1)}, f32[48]{0:T(128)}, u32[]{:S(2)}) copy-start(f32[48]{0:T(128)} %get-tuple-element.448) | copy-start | bytes 580
  92.4 7.0 %collective-permute-start.3 = (bf16[48,1536]{1,0:T(8,128)(2,1)S(1)}, bf16[48,1536]{1,0:T(8,128)(2,1)S(1)}, u32[]{:S(2)}, u32[]{:S(2)}) collective-permute-start(bf16[48,1536]{1,0:T(8,128)(2,1)S(1)} %get-tuple-element.422), channel_id=1, source_target_pairs={{64,0},{128,64},{192,128},{65,1},{129,65},{193,129},{66,2},{130,66... | collective-permute-start | bytes 442376 | tf_op jit(solution)/shard_map/ppermute | solution.py:12
  102.7 8.7 %copy-start.142 = (f32[48]{0:T(128)S(1)}, f32[48]{0:T(128)}, u32[]{:S(2)}) copy-start(f32[48]{0:T(128)} %get-tuple-element.447) | copy-start | bytes 580
  104.3 7.0 %collective-permute-start.4 = (bf16[48,1536]{1,0:T(8,128)(2,1)S(1)}, bf16[48,1536]{1,0:T(8,128)(2,1)S(1)}, u32[]{:S(2)}, u32[]{:S(2)}) collective-permute-start(bf16[48,1536]{1,0:T(8,128)(2,1)S(1)} %get-tuple-element.420), channel_id=1, source_target_pairs={{64,0},{128,64},{192,128},{65,1},{129,65},{193,129},{66,2},{130,66... | collective-permute-start | bytes 442376 | tf_op jit(solution)/shard_map/ppermute | solution.py:12
  114.6 8.7 %copy-start.140 = (f32[48]{0:T(128)S(1)}, f32[48]{0:T(128)}, u32[]{:S(2)}) copy-start(f32[48]{0:T(128)} %get-tuple-element.446) | copy-start | bytes 580
  116.2 7.0 %collective-permute-start.5 = (bf16[48,1536]{1,0:T(8,128)(2,1)S(1)}, bf16[48,1536]{1,0:T(8,128)(2,1)S(1)}, u32[]{:S(2)}, u32[]{:S(2)}) collective-permute-start(bf16[48,1536]{1,0:T(8,128)(2,1)S(1)} %get-tuple-element.418), channel_id=1, source_target_pairs={{64,0},{128,64},{192,128},{65,1},{129,65},{193,129},{66,2},{130,66... | collective-permute-start | bytes 442376 | tf_op jit(solution)/shard_map/ppermute | solution.py:12
  142.9 345.4 %reduce-scatter.2.cloned.1.call-start = ((), (), s32[]{:S(2)}) async-start(), calls=%async_computation.1 | async-start | bytes 9584640 | tf_op jit(solution)/shard_map/reduce_scatter | solution.py:114
  151.9 337.9 %copy-start.9 = (bf16[4,48,1536]{2,1,0:T(8,128)(2,1)}, bf16[4,48,1536]{2,1,0:T(8,128)(2,1)S(1)}, u32[]{:S(2)}) copy-start(bf16[4,48,1536]{2,1,0:T(8,128)(2,1)S(1)} %fusion.520) | copy-start | bytes 1769476
  (121 other events, 216.5 us)
Sparse Core Ops, SparseCore 0:
  143.0 186.6 all-reduce.10
  334.0 154.2 reduce-scatter.1
